TPU v7x, 256 devices: a whole 4x4x8 slice. The times are simulated.
256 devices in a mesh: band: 8 (over x_hi, y), dom: 32 (over x_lo, z, core).
Axes of the slice: x: 4 (x_hi: 2, x_lo: 2; x = x_hi * 2 + x_lo), y: 4, z: 8, core: 2. Of those that a mesh axis runs over, the one named last changes fastest.
Arguments:
- wave: bfloat16 [192, 19, 13, 2048], P('dom', None, None, 'band'), parts along dimension 3, may hold values from -6 to 6
- kinetic: bfloat16 [343, 343], replicated, may hold values from -1 to 1, as said below
- cell_scale: float32 [192], P('dom'), may hold values from 0.5 to 2
- potential: float32 [192, 19, 13], P('dom'), may hold values from 0.2 to 2
- proj_values: bfloat16 [512, 343], P('dom'), may hold values from -0.23925781 to 0.23925781
- piece_cell: int32 [512], P('dom'), may hold values from 0 to 5
- piece_proj: int32 [512], P('dom'), may hold values from 0 to 255
- coupling: float32 [256], replicated, may hold values from 0.5 to 2
- center: float32 [1], replicated, may hold values from 9 to 11
- halfwidth: float32 [1], replicated, may hold values from 14 to 18
Outputs:
- filtered: float32 [192, 19, 13, 2048], P('dom', None, None, 'band'), parts along dimension 3
There are 8 independent parts, one for each index of `band`. A program takes and returns all parts, laid end to end along the dimension named above; an argument that names none is the same for every part. Nothing has to cross between parts.
Inputs may be any that keep to these rules, and one draw needn't show every extreme that they name: kinetic is symmetric.
All inputs are finite; a program needn't handle non-finite values.
Results may differ from a plain program's by a relative error of at most 0.0014.
Values may be sent and summed in bfloat16 or wider, within the bound.
No kernel may reach another device: no remote copies, remote signals or barrier semaphores. Data moves between devices by JAX's collectives and lax.ppermute only.
A program may use at most 64 MiB of HBM per device.

v0:
```python
import jax
import jax.numpy as jnp
from jax import lax
from jax.sharding import PartitionSpec as P

P_SIZE = 7
CXC = 2
CYC = 3
CZC = 1
NPROJ = 256
DEGREE = 4


def passed_along(value, axis, steps):
    count = lax.axis_size(axis)
    pairs = [(source, (source + steps) % count) for source in range(count)]
    return lax.ppermute(value, axis, pairs)


def spread_axis(field, axis, count):
    span = (P_SIZE - 1) * (count - 1) + 1
    slices = [
        lax.slice_in_dim(field, start, start + span, stride=P_SIZE - 1, axis=axis)
        for start in range(P_SIZE)
    ]
    return jnp.stack(slices, axis=axis + 1)


def extract(extended):
    width = extended.shape[3]
    gathered = spread_axis(extended, 2, CXC)
    gathered = spread_axis(gathered, 1, CYC)
    gathered = spread_axis(gathered, 0, CZC)
    gathered = gathered.transpose(0, 2, 4, 1, 3, 5, 6)
    return gathered.reshape(CZC * CYC * CXC, P_SIZE * P_SIZE * P_SIZE, width)


def fold_front(grouped):
    count = grouped.shape[0]
    rest = grouped.shape[2:]
    heads = grouped[:, : P_SIZE - 1]
    tails = grouped[:, P_SIZE - 1 :]
    moved = jnp.concatenate([tails, jnp.zeros((count, P_SIZE - 2) + rest, jnp.float32)], axis=1)
    empty = jnp.zeros((1, P_SIZE - 1) + rest, jnp.float32)
    total = jnp.concatenate([heads, empty], axis=0) + jnp.concatenate([empty, moved], axis=0)
    total = total.reshape(((count + 1) * (P_SIZE - 1),) + rest)
    return total[: count * (P_SIZE - 1) + 1]


def fold_axis(grouped, axis):
    moved = jnp.moveaxis(grouped, (axis, axis + 1), (0, 1))
    return jnp.moveaxis(fold_front(moved), 0, axis)


def assemble(cell_out):
    width = cell_out.shape[2]
    grouped = cell_out.reshape(CZC, CYC, CXC, P_SIZE, P_SIZE, P_SIZE, width).transpose(
        0, 3, 1, 4, 2, 5, 6
    )
    grouped = fold_axis(grouped, 4)
    grouped = fold_axis(grouped, 2)
    return fold_axis(grouped, 0)


def apply_hamiltonian(
    current,
    kinetic,
    cell_scale,
    potential,
    proj_values,
    piece_cell,
    piece_proj,
    coupling,
    center,
    halfwidth,
):
    rounded = current.astype(jnp.bfloat16)
    neighbour = passed_along(rounded[0:1], "dom", -1)
    extended = jnp.concatenate([rounded, neighbour], axis=0)
    cell_vals = extract(extended)
    cell_out = (
        jnp.einsum("pq,nqk->npk", kinetic, cell_vals, preferred_element_type=jnp.float32)
        * cell_scale[:, None, None]
    )
    picked = jnp.take(cell_vals, piece_cell, axis=0)
    piece_coef = jnp.einsum("np,npk->nk", proj_values, picked, preferred_element_type=jnp.float32)
    proj_hot = piece_proj[None, :] == jnp.arange(NPROJ, dtype=jnp.int32)[:, None]
    partial_coef = jnp.dot(
        proj_hot.astype(jnp.float32), piece_coef, precision=lax.Precision.HIGHEST
    )
    summed = lax.psum(partial_coef.astype(jnp.bfloat16), "dom").astype(jnp.float32)
    scaled = (coupling[:, None] * summed).astype(jnp.bfloat16)
    per_piece = jnp.dot(proj_hot.T.astype(jnp.bfloat16), scaled, preferred_element_type=jnp.float32)
    weighted = proj_values.astype(jnp.float32)[:, :, None] * per_piece[:, None, :]
    cell_hot = (
        piece_cell[None, :] == jnp.arange(cell_vals.shape[0], dtype=jnp.int32)[:, None]
    ).astype(jnp.float32)
    cell_out = cell_out + jnp.einsum(
        "mn,npk->mpk", cell_hot, weighted, precision=lax.Precision.HIGHEST
    )
    assembled = assemble(cell_out)
    shared = passed_along(assembled[-1:], "dom", 1)
    applied = jnp.concatenate([assembled[0:1] + shared, assembled[1:-1]], axis=0)
    return (applied + (potential[..., None] - center[0]) * current) / halfwidth[0]


def filter_block(block, operands):
    previous = block.astype(jnp.float32)
    current = apply_hamiltonian(previous, *operands)
    for step in range(DEGREE - 1):
        following = 2.0 * apply_hamiltonian(current, *operands) - previous
        previous = current
        current = following
    return current


def local(
    wave,
    kinetic,
    cell_scale,
    potential,
    proj_values,
    piece_cell,
    piece_proj,
    coupling,
    center,
    halfwidth,
):
    operands = (
        kinetic,
        cell_scale,
        potential,
        proj_values,
        piece_cell,
        piece_proj,
        coupling,
        center,
        halfwidth,
    )
    half_cols = wave.shape[3] // 2
    first = filter_block(wave[..., :half_cols], operands)
    second = filter_block(wave[..., half_cols:], operands)
    return jnp.concatenate([first, second], axis=3)


def solution(mesh):
    in_specs = (
        P("dom", None, None, "band"),
        P(),
        P("dom"),
        P("dom", None, None),
        P("dom", None),
        P("dom"),
        P("dom"),
        P(),
        P(),
        P(),
    )
    out_specs = P("dom", None, None, "band")
    return jax.shard_map(local, mesh=mesh, in_specs=in_specs, out_specs=out_specs, check_vma=False)
```

profile of v0, /device:TPU:6, one launch (start us, length us, event | category | flops | bytes accessed | tf_op | source)
XLA Modules:
  0.0 1327.0 jit_solution(2562481858828304736)
XLA Ops:
  7.5 5.6 collective-permute-start
  36.4 200.5 %all-reduce.87.cloned.1.call-done = (bf16[256,128]{1,0:T(8,128)(2,1)}, bf16[256,128]{1,0:T(8,128)(2,1)}) async-done(((bf16[256,128]{1,0:T(8,128)(2,1)}, bf16[256,128]{1,0:T(8,128)(2,1)}), (bf16[256,128]{1,0:T(8,128)(2,1)}, bf16[256,128]{1,0:T(8,128)(2,1)})) %all-reduce.87.cloned.1.call-update) | async-done | bytes 131088 | tf_op jit(solution)/shard_map/psum | solution.py:91
  258.6 5.9 collective-permute-done.1
  269.8 4.6 slice.1062
  274.4 4.6 slice.1061
  278.9 4.5 slice.1060
  283.5 4.5 slice.1059
  288.0 4.5 slice.1058
  292.6 4.5 slice.1057
  297.1 4.2 slice.1056
  303.1 4.5 slice.929
  307.6 4.5 slice.928
  312.2 4.6 slice.927
  316.7 4.5 slice.926
  321.3 4.5 slice.925
  325.8 4.5 slice.924
  330.4 3.2 slice.923
  361.1 2.5 reshape.280
  365.6 2.9 gather_fusion.1
  375.9 202.4 %all-reduce.85.cloned.1.call-done = (bf16[256,128]{1,0:T(8,128)(2,1)}, bf16[256,128]{1,0:T(8,128)(2,1)}) async-done(((bf16[256,128]{1,0:T(8,128)(2,1)}, bf16[256,128]{1,0:T(8,128)(2,1)}), (bf16[256,128]{1,0:T(8,128)(2,1)}, bf16[256,128]{1,0:T(8,128)(2,1)})) %all-reduce.85.cloned.1.call-update) | async-done | bytes 131088 | tf_op jit(solution)/shard_map/psum | solution.py:91
  579.5 2.2 fusion.12
  583.2 2.4 reshape.146
  597.5 2.4 reshape.166
  608.3 5.9 collective-permute-done.3
  620.8 4.6 slice.1095
  625.4 4.6 slice.1094
  630.0 4.5 slice.1093
  634.5 4.5 slice.1092
  639.0 4.5 slice.1091
  643.6 4.5 slice.1090
  648.1 4.2 slice.1089
  654.1 4.5 slice.962
  658.6 4.5 slice.961
  663.2 4.6 slice.960
  667.7 4.5 slice.959
  672.3 4.5 slice.958
  676.8 4.5 slice.957
  681.4 3.2 slice.956
  712.1 2.5 reshape.281
  716.6 2.9 gather_fusion.2
  726.8 202.7 %all-reduce.83.cloned.1.call-done = (bf16[256,128]{1,0:T(8,128)(2,1)}, bf16[256,128]{1,0:T(8,128)(2,1)}) async-done(((bf16[256,128]{1,0:T(8,128)(2,1)}, bf16[256,128]{1,0:T(8,128)(2,1)}), (bf16[256,128]{1,0:T(8,128)(2,1)}, bf16[256,128]{1,0:T(8,128)(2,1)})) %all-reduce.83.cloned.1.call-update) | async-done | bytes 131088 | tf_op jit(solution)/shard_map/psum | solution.py:91
  934.2 2.4 reshape.151
  948.5 2.4 reshape.171
  959.6 5.9 collective-permute-done.5
  971.3 4.5 slice.1128
  975.8 4.5 slice.1127
  980.3 4.5 slice.1126
  984.9 4.5 slice.1125
  989.4 4.5 slice.1124
  994.0 4.5 slice.1123
  998.5 4.2 slice.1122
  1004.5 4.5 slice.995
  1009.0 4.6 slice.994
  1013.6 4.6 slice.993
  1018.1 4.5 slice.992
  1022.7 4.5 slice.991
  1027.2 4.6 slice.990
  1031.8 3.2 slice.989
  1062.5 2.7 reshape.282
  1067.2 2.9 gather_fusion.3
  1077.1 202.9 %all-reduce.81.cloned.1.call-done = (bf16[256,128]{1,0:T(8,128)(2,1)}, bf16[256,128]{1,0:T(8,128)(2,1)}) async-done(((bf16[256,128]{1,0:T(8,128)(2,1)}, bf16[256,128]{1,0:T(8,128)(2,1)}), (bf16[256,128]{1,0:T(8,128)(2,1)}, bf16[256,128]{1,0:T(8,128)(2,1)})) %all-reduce.81.cloned.1.call-update) | async-done | bytes 131088 | tf_op jit(solution)/shard_map/psum | solution.py:91
  1284.8 2.4 reshape.156
  1299.1 2.4 reshape.176
  1309.9 5.9 collective-permute-done.7
  (542 shorter events, 253.6 us)
Async XLA Ops:
  6.5 232.8 %copy-start = (bf16[343,343]{1,0:T(8,128)(2,1)S(1)}, bf16[343,343]{1,0:T(8,128)(2,1)}, u32[]{:S(2)}) copy-start(bf16[343,343]{1,0:T(8,128)(2,1)} %param.13) | copy-start | bytes 705898
  6.5 11.3 copy-start.53
  6.5 230.3 %all-reduce.87.cloned.1.call-start = ((), (), s32[]{:S(2)}) async-start(), calls=%async_computation.3 | async-start | bytes 262144 | tf_op jit(solution)/shard_map/psum | solution.py:91
  7.5 10.4 collective-permute-start
  13.2 4.8 collective-permute-start.8
  17.9 231.4 %copy-start.43 = (f32[16,343]{0,1:T(8,128)}, f32[16,343]{0,1:T(8,128)S(1)}, u32[]{:S(2)}) copy-start(f32[16,343]{0,1:T(8,128)S(1)} %copy.84) | copy-start | bytes 65860
  33.4 2.8 copy-start.50
  33.4 203.5 %copy-start.58 = (f32[256]{0:T(256)S(1)}, f32[256]{0:T(256)}, u32[]{:S(2)}) copy-start(f32[256]{0:T(256)} %param.19) | copy-start | bytes 3076
  33.4 204.6 %copy-start.59 = (s32[16]{0:T(128)S(1)}, s32[16]{0:T(128)}, u32[]{:S(2)}) copy-start(s32[16]{0:T(128)} %param.17) | copy-start | bytes 196
  35.7 542.7 %all-reduce.85.cloned.1.call-start = ((), (), s32[]{:S(2)}) async-start(), calls=%async_computation.2 | async-start | bytes 262144 | tf_op jit(solution)/shard_map/psum | solution.py:91
  36.4 202.9 %copy-start.52 = (f32[6]{0:T(128)S(1)}, f32[6]{0:T(128)}, u32[]{:S(2)}) copy-start(f32[6]{0:T(128)} %param.14) | copy-start | bytes 76
  257.7 6.8 collective-permute-start.1
  258.4 7.8 copy-start.1
  258.5 7.7 collective-permute-start.9
  266.9 2.0 collective-permute-start.10
  267.5 33.8 %collective-permute-start.2 = (bf16[1,19,13,128]{3,2,1,0:T(8,128)(2,1)}, bf16[1,19,13,128]{3,2,1,0:T(8,128)(2,1)}, u32[]{:S(2)}, u32[]{:S(2)}) collective-permute-start(bf16[1,19,13,128]{3,2,1,0:T(8,128)(2,1)} %slice.1188), channel_id=1, source_target_pairs={{0,31},{1,0},{2,1},{3,2},{4,3},{5,4},{6,5},{7,6},{8,7},{9,8},{10,9... | collective-permute-start | bytes 189704 | tf_op jit(solution)/shard_map/ppermute | solution.py:17
  343.4 2.8 copy-start.40
  343.5 3.5 copy-start.37
  343.5 4.2 copy-start.34
  343.5 4.8 copy-start.31
  343.5 5.5 copy-start.28
  375.5 553.9 %all-reduce.83.cloned.1.call-start = ((), (), s32[]{:S(2)}) async-start(), calls=%async_computation.1 | async-start | bytes 262144 | tf_op jit(solution)/shard_map/psum | solution.py:91
  578.4 3.4 copy-start.2
  592.8 3.2 copy-start.15
  607.4 6.8 collective-permute-start.3
  608.1 7.8 copy-start.18
  608.1 7.8 copy-start.22
  608.2 7.7 collective-permute-start.11
  617.8 2.1 collective-permute-start.12
  618.6 33.8 %collective-permute-start.4 = (bf16[1,19,13,128]{3,2,1,0:T(8,128)(2,1)}, bf16[1,19,13,128]{3,2,1,0:T(8,128)(2,1)}, u32[]{:S(2)}, u32[]{:S(2)}) collective-permute-start(bf16[1,19,13,128]{3,2,1,0:T(8,128)(2,1)} %slice.1207), channel_id=1, source_target_pairs={{0,31},{1,0},{2,1},{3,2},{4,3},{5,4},{6,5},{7,6},{8,7},{9,8},{10,9... | collective-permute-start | bytes 189704 | tf_op jit(solution)/shard_map/ppermute | solution.py:17
  694.5 2.8 copy-start.41
  694.5 3.5 copy-start.38
  694.5 4.2 copy-start.35
  694.5 4.8 copy-start.32
  694.5 5.5 copy-start.29
  726.5 553.5 %all-reduce.81.cloned.1.call-start = ((), (), s32[]{:S(2)}) async-start(), calls=%async_computation | async-start | bytes 262144 | tf_op jit(solution)/shard_map/psum | solution.py:91
  929.4 3.4 copy-start.3
  943.8 3.2 copy-start.16
  958.7 6.8 collective-permute-start.5
  959.4 7.8 copy-start.5
  959.4 7.8 copy-start.7
  959.4 7.8 copy-start.9
  959.4 7.8 copy-start.19
  959.5 8.8 copy-start.11
  959.5 7.7 collective-permute-start.13
  968.3 2.1 collective-permute-start.14
  969.0 33.7 %collective-permute-start.6 = (bf16[1,19,13,128]{3,2,1,0:T(8,128)(2,1)}, bf16[1,19,13,128]{3,2,1,0:T(8,128)(2,1)}, u32[]{:S(2)}, u32[]{:S(2)}) collective-permute-start(bf16[1,19,13,128]{3,2,1,0:T(8,128)(2,1)} %slice.1226), channel_id=1, source_target_pairs={{0,31},{1,0},{2,1},{3,2},{4,3},{5,4},{6,5},{7,6},{8,7},{9,8},{10,9... | collective-permute-start | bytes 189704 | tf_op jit(solution)/shard_map/ppermute | solution.py:17
  1044.9 2.8 copy-start.42
  1044.9 3.5 copy-start.39
  1044.9 4.2 copy-start.36
  1044.9 4.8 copy-start.33
  1044.9 5.5 copy-start.30
  1280.0 3.4 copy-start.4
  1294.4 3.2 copy-start.13
  1309.1 6.8 collective-permute-start.7
  1309.2 8.3 copy-start.12
  1309.2 8.3 copy-start.21
  1309.2 8.3 copy-start.25
  1309.2 8.3 copy-start.27
  1309.7 7.8 copy-start.6
  1309.7 7.8 copy-start.8
  1309.8 7.8 copy-start.10
  1309.8 7.8 copy-start.20
  1309.9 7.6 collective-permute-start.15
  (16 other events, 22.7 us)
Sparse Core Ops, SparseCore 0:
  35.8 201.0 all-reduce.86
  375.6 202.7 all-reduce.84
  726.6 202.7 all-reduce.82
  1077.2 202.7 all-reduce.80
where the time goes:
time: 1350 us; the launch traced here: 1330 us
  waiting for transfers between devices  838 us (62%)
  local copies, waits for them, and re-layouts  377 us (28%)
  matrix products  48.8 us (4%)
  other arithmetic  36.6 us (3%)
  between operations  16.8 us (1%)
    psum x4, waiting for transfers between devices, apply_hamiltonian(): lax.psum(partial_coef.astype(jnp.bfloat16), 'dom').astype(jnp.float32)  809 us
    slice x56, local copies, waits for them, and re-layouts, spread_axis(): lax.slice_in_dim(field, start, start + span, stride=P_SIZE - 1, axis=axis)  191 us
    unnamed x264, local copies, waits for them, and re-layouts  69.5 us
    ppermute x16, waiting for transfers between devices, passed_along(): return lax.ppermute(value, axis, pairs)  29.7 us
  transfers between devices with their start and end apart: 20, of which 15 were waited for; matrix products, arithmetic and copies ran while one was open for 8% of the time, Pallas kernels for 0%

commit v1 on v0

--- a/solution.py
+++ b/solution.py
@@ -88,7 +88,8 @@
     partial_coef = jnp.dot(
         proj_hot.astype(jnp.float32), piece_coef, precision=lax.Precision.HIGHEST
     )
-    summed = lax.psum(partial_coef.astype(jnp.bfloat16), "dom").astype(jnp.float32)
+    push_leaf_all = lambda body, shard_axis: jnp.sum(lax.all_gather(body, axis_name=shard_axis), 0)
+    summed = push_leaf_all(partial_coef.astype(jnp.bfloat16), "dom").astype(jnp.float32)
     scaled = (coupling[:, None] * summed).astype(jnp.bfloat16)
     per_piece = jnp.dot(proj_hot.T.astype(jnp.bfloat16), scaled, preferred_element_type=jnp.float32)
     weighted = proj_values.astype(jnp.float32)[:, :, None] * per_piece[:, None, :]

time: 1350 us -> 838 us (0.62)
  waiting for transfers between devices: 838 us -> 472 us
  local copies, waits for them, and re-layouts: 377 us -> 234 us
    psum x4 -> x0, waiting for transfers between devices: 809 us -> none  [apply_hamiltonian(): lax.psum(partial_coef.astype(jnp.bfloat16), 'dom').astype(jnp.float32)]
    all_gather x0 -> x8, waiting for transfers between devices: none -> 422 us  [apply_hamiltonian(): lax.all_gather(body, axis_name=shard_axis)]
    slice x56, local copies, waits for them, and re-layouts: 191 us -> 109 us  [spread_axis(): lax.slice_in_dim(field, start, start + span, stride=P_SIZE - 1, axis=axis)]
    unnamed x264 -> x224, local copies, waits for them, and re-layouts: 69.5 us -> 31.7 us
    ppermute x16, waiting for transfers between devices: 29.7 us -> 49.4 us  [passed_along(): return lax.ppermute(value, axis, pairs)]
    reduce_sum x0 -> x8, other arithmetic: none -> 16.3 us  [apply_hamiltonian(): jnp.sum(lax.all_gather(body, axis_name=shard_axis), 0)]
  transfers between devices with their start and end apart: 20 -> 24, of which waited for: 15 -> 20; matrix products, arithmetic and copies ran while one was open for 8% -> 15% of each run, Pallas kernels for 0% -> 0%
where the time goes in v1:
time: 838 us; the launch traced here: 826 us
  waiting for transfers between devices  472 us (56%)
  local copies, waits for them, and re-layouts  234 us (28%)
  other arithmetic  46.8 us (6%)
  matrix products  44.7 us (5%)
  between operations  17.4 us (2%)
  starting transfers between devices  11.4 us (1%)
    all_gather x8, waiting for transfers between devices, apply_hamiltonian(): lax.all_gather(body, axis_name=shard_axis)  422 us
    slice x56, local copies, waits for them, and re-layouts, spread_axis(): lax.slice_in_dim(field, start, start + span, stride=P_SIZE - 1, axis=axis)  109 us
    ppermute x16, waiting for transfers between devices, passed_along(): return lax.ppermute(value, axis, pairs)  49.4 us
    unnamed x224, local copies, waits for them, and re-layouts  31.7 us
    reshape x16, local copies, waits for them, and re-layouts, extract(): return gathered.reshape(CZC * CYC * CXC, P_SIZE * P_SIZE * P_SIZE, width)  18.7 us
  transfers between devices with their start and end apart: 24, of which 20 were waited for; matrix products, arithmetic and copies ran while one was open for 15% of the time, Pallas kernels for 0%

profile of v1, /device:TPU:6, one launch (start us, length us, event | category | flops | bytes accessed | tf_op | source)
XLA Modules:
  0.0 825.8 jit_solution(13623882807178044205)
XLA Ops:
  7.5 5.6 collective-permute-start
  26.6 61.0 %all-gather.17.cloned.1.call-done = bf16[8192,128]{1,0:T(8,128)(2,1)} async-done(((bf16[256,128]{1,0:T(8,128)(2,1)}), bf16[8192,128]{1,0:T(8,128)(2,1)}) %all-gather.17.cloned.1.call-update) | async-done | bytes 2097168 | tf_op jit(solution)/shard_map/all_gather | solution.py:91
  87.7 1.9 reduce_sum.96
  99.0 4.3 collective-permute-done.1
  104.9 2.0 collective-permute-done.2
  108.5 2.5 slice.925
  111.0 2.5 slice.924
  113.6 2.5 slice.923
  121.0 1.8 gather_fusion.1
  125.5 4.6 slice.1025
  130.1 4.6 slice.1024
  134.7 3.2 slice.1023
  138.6 50.5 %all-gather.19.cloned.1.call-done = bf16[8192,128]{1,0:T(8,128)(2,1)} async-done(((bf16[256,128]{1,0:T(8,128)(2,1)}), bf16[8192,128]{1,0:T(8,128)(2,1)}) %all-gather.19.cloned.1.call-update) | async-done | bytes 2097168 | tf_op jit(solution)/shard_map/all_gather | solution.py:91
  189.1 1.9 reduce_sum.97
  201.1 5.8 collective-permute-done.3
  209.1 4.5 slice.1029
  213.6 4.6 slice.1028
  218.1 4.5 slice.1027
  222.7 4.6 slice.1026
  234.1 1.8 gather_fusion.2
  251.8 1.8 gather_fusion.4
  253.6 48.4 %all-gather.21.cloned.1.call-done = bf16[8192,128]{1,0:T(8,128)(2,1)} async-done(((bf16[256,128]{1,0:T(8,128)(2,1)}), bf16[8192,128]{1,0:T(8,128)(2,1)}) %all-gather.21.cloned.1.call-update) | async-done | bytes 2097168 | tf_op jit(solution)/shard_map/all_gather | solution.py:91
  302.0 1.9 reduce_sum.98
  307.0 2.4 reshape.151
  317.9 5.5 collective-permute-done.5
  327.1 3.7 slice.995
  330.8 3.7 slice.994
  334.5 3.7 slice.993
  338.2 3.7 slice.992
  341.9 4.6 slice.991
  346.5 4.5 slice.990
  351.1 4.2 slice.989
  362.1 1.8 gather_fusion.3
  366.6 21.8 %all-gather.25.cloned.1.call-done = bf16[8192,128]{1,0:T(8,128)(2,1)} async-done(((bf16[256,128]{1,0:T(8,128)(2,1)}), bf16[8192,128]{1,0:T(8,128)(2,1)}) %all-gather.25.cloned.1.call-update) | async-done | bytes 2097168 | tf_op jit(solution)/shard_map/all_gather | solution.py:91
  388.4 1.9 reduce_sum.100
  393.3 2.4 reshape.161
  404.8 49.5 %all-gather.23.cloned.1.call-done = bf16[8192,128]{1,0:T(8,128)(2,1)} async-done(((bf16[256,128]{1,0:T(8,128)(2,1)}), bf16[8192,128]{1,0:T(8,128)(2,1)}) %all-gather.23.cloned.1.call-update) | async-done | bytes 2097168 | tf_op jit(solution)/shard_map/all_gather | solution.py:91
  454.3 2.5 reduce_sum.99
  457.9 2.2 fusion.8
  461.6 2.4 reshape.156
  472.8 5.3 collective-permute-done.7
  480.3 2.0 collective-permute-done.10
  493.7 63.6 %all-gather.27.cloned.1.call-done = bf16[8192,128]{1,0:T(8,128)(2,1)} async-done(((bf16[256,128]{1,0:T(8,128)(2,1)}), bf16[8192,128]{1,0:T(8,128)(2,1)}) %all-gather.27.cloned.1.call-update) | async-done | bytes 2097168 | tf_op jit(solution)/shard_map/all_gather | solution.py:91
  557.3 1.9 reduce_sum.101
  562.2 2.4 reshape.166
  572.2 6.5 collective-permute-done.11
  580.3 2.0 collective-permute-done.12
  593.7 63.6 %all-gather.29.cloned.1.call-done = bf16[8192,128]{1,0:T(8,128)(2,1)} async-done(((bf16[256,128]{1,0:T(8,128)(2,1)}), bf16[8192,128]{1,0:T(8,128)(2,1)}) %all-gather.29.cloned.1.call-update) | async-done | bytes 2097168 | tf_op jit(solution)/shard_map/all_gather | solution.py:91
  657.3 1.9 reduce_sum.102
  662.2 2.4 reshape.171
  672.4 6.5 collective-permute-done.13
  679.5 2.0 collective-permute-done.14
  682.4 4.5 slice.1128
  687.0 4.5 slice.1127
  691.5 4.5 slice.1126
  696.1 4.5 slice.1125
  700.6 4.5 slice.1124
  705.2 4.5 slice.1123
  709.7 4.2 slice.1122
  728.7 63.6 %all-gather.31.cloned.1.call-done = bf16[8192,128]{1,0:T(8,128)(2,1)} async-done(((bf16[256,128]{1,0:T(8,128)(2,1)}), bf16[8192,128]{1,0:T(8,128)(2,1)}) %all-gather.31.cloned.1.call-update) | async-done | bytes 2097168 | tf_op jit(solution)/shard_map/all_gather | solution.py:91
  792.4 2.5 reduce_sum.103
  795.9 2.2 fusion
  799.6 2.4 reshape.176
  809.6 6.5 collective-permute-done.15
  (525 shorter events, 192.1 us)
Async XLA Ops:
  6.5 84.6 %copy-start = (bf16[343,343]{1,0:T(8,128)(2,1)S(1)}, bf16[343,343]{1,0:T(8,128)(2,1)}, u32[]{:S(2)}) copy-start(bf16[343,343]{1,0:T(8,128)(2,1)} %param.13) | copy-start | bytes 705898
  6.5 81.1 %all-gather.17.cloned.1.call-start = ((), (), s32[]{:S(2)}) async-start(), calls=%async_computation | async-start | bytes 2162688 | tf_op jit(solution)/shard_map/all_gather | solution.py:91
  7.5 9.0 %collective-permute-start = (bf16[1,19,13,128]{3,2,1,0:T(8,128)(2,1)S(1)}, bf16[1,19,13,128]{3,2,1,0:T(8,128)(2,1)S(1)}, u32[]{:S(2)}, u32[]{:S(2)}) collective-permute-start(bf16[1,19,13,128]{3,2,1,0:T(8,128)(2,1)S(1)} %get-tuple-element.14), channel_id=1, source_target_pairs={{0,31},{1,0},{2,1},{3,2},{4,3},{5,4},{6,5},{7,6},{8,7},{9,8},{10,9... | collective-permute-start | bytes 189704 | tf_op jit(solution)/shard_map/ppermute | solution.py:17
  13.2 3.4 collective-permute-start.8
  14.5 8.7 %copy-start.35 = (pred[16]{0:T(512)(128)(4,1)}, pred[16]{0:T(512)(128)(4,1)S(1)}, u32[]{:S(2)}) copy-start(pred[16]{0:T(512)(128)(4,1)S(1)} %compare_and_fusion) | copy-start | bytes 52
  22.3 0.9 copy-start.30
  23.2 0.7 copy-start.28
  23.6 65.9 %copy-start.33 = (f32[256]{0:T(256)S(1)}, f32[256]{0:T(256)}, u32[]{:S(2)}) copy-start(f32[256]{0:T(256)} %param.19) | copy-start | bytes 3076
  23.6 66.2 %copy-start.34 = (s32[16]{0:T(128)S(1)}, s32[16]{0:T(128)}, u32[]{:S(2)}) copy-start(s32[16]{0:T(128)} %param.17) | copy-start | bytes 196
  24.7 164.4 %all-gather.19.cloned.1.call-start = ((), (), s32[]{:S(2)}) async-start(), calls=%async_computation.1 | async-start | bytes 2162688 | tf_op jit(solution)/shard_map/all_gather | solution.py:91
  25.3 65.8 %copy-start.22 = (f32[16,343]{0,1:T(8,128)}, f32[16,343]{0,1:T(8,128)S(1)}, u32[]{:S(2)}) copy-start(f32[16,343]{0,1:T(8,128)S(1)} %copy.84) | copy-start | bytes 65860
  89.5 1.6 copy-start.29
  95.9 1.8 copy-start.27
  96.4 1.2 copy-start.9
  96.5 7.8 copy-start.1
  96.5 6.8 collective-permute-start.1
  104.6 2.3 collective-permute-start.2
  121.0 1.8 copy-start.36
  125.5 176.6 %all-gather.21.cloned.1.call-start = ((), (), s32[]{:S(2)}) async-start(), calls=%async_computation.2 | async-start | bytes 2162688 | tf_op jit(solution)/shard_map/all_gather | solution.py:91
  125.5 65.7 %copy-start.23 = (f32[16,343]{0,1:T(8,128)S(1)}, f32[16,343]{0,1:T(8,128)}, u32[]{:S(2)}) copy-start(f32[16,343]{0,1:T(8,128)} %copy-done.22) | copy-start | bytes 65860
  199.5 0.9 copy-start.21
  200.1 6.8 collective-permute-start.3
  206.9 1.4 copy-start.20
  208.4 18.9 %collective-permute-start.4 = (bf16[1,19,13,128]{3,2,1,0:T(8,128)(2,1)S(1)}, bf16[1,19,13,128]{3,2,1,0:T(8,128)(2,1)S(1)}, u32[]{:S(2)}, u32[]{:S(2)}) collective-permute-start(bf16[1,19,13,128]{3,2,1,0:T(8,128)(2,1)S(1)} %slice.1207), channel_id=1, source_target_pairs={{0,31},{1,0},{2,1},{3,2},{4,3},{5,4},{6,5},{7,6},{8,7},{9,8},{10,9... | collective-permute-start | bytes 189704 | tf_op jit(solution)/shard_map/ppermute | solution.py:17
  236.0 3.1 copy-start.19
  236.0 3.8 copy-start.18
  236.0 4.5 copy-start.17
  236.0 5.2 copy-start.16
  238.6 149.8 %all-gather.25.cloned.1.call-start = ((), (), s32[]{:S(2)}) async-start(), calls=%async_computation.4 | async-start | bytes 2162688 | tf_op jit(solution)/shard_map/all_gather | solution.py:91
  253.6 50.6 %copy-start.24 = (f32[16,343]{0,1:T(8,128)S(1)}, f32[16,343]{0,1:T(8,128)}, u32[]{:S(2)}) copy-start(f32[16,343]{0,1:T(8,128)} %copy-done.22) | copy-start | bytes 65860
  316.1 1.4 copy-start.13
  316.1 1.3 copy-start.37
  316.6 6.8 collective-permute-start.5
  317.8 5.7 copy-start.2
  317.9 6.1 copy-start.6
  323.5 0.7 copy-start.14
  324.1 2.0 collective-permute-start.6
  325.0 129.3 %all-gather.23.cloned.1.call-start = ((), (), s32[]{:S(2)}) async-start(), calls=%async_computation.3 | async-start | bytes 2162688 | tf_op jit(solution)/shard_map/all_gather | solution.py:91
  362.1 1.8 copy-start.38
  365.7 24.8 %copy-start.25 = (f32[16,343]{0,1:T(8,128)S(1)}, f32[16,343]{0,1:T(8,128)}, u32[]{:S(2)}) copy-start(f32[16,343]{0,1:T(8,128)} %copy-done.22) | copy-start | bytes 65860
  366.6 190.7 %all-gather.27.cloned.1.call-start = ((), (), s32[]{:S(2)}) async-start(), calls=%async_computation.5 | async-start | bytes 2162688 | tf_op jit(solution)/shard_map/all_gather | solution.py:91
  402.9 1.3 copy-start.8
  404.3 67.3 %collective-permute-start.9 = (f32[1,19,13,128]{3,2,1,0:T(8,128)}, f32[1,19,13,128]{3,2,1,0:T(8,128)}, u32[]{:S(2)}, u32[]{:S(2)}) collective-permute-start(f32[1,19,13,128]{3,2,1,0:T(8,128)} %slice.1261), channel_id=1, source_target_pairs={{0,1},{1,2},{2,3},{3,4},{4,5},{5,6},{6,7},{7,8},{8,9},{9,10},{10,1... | collective-permute-start | bytes 379400 | tf_op jit(solution)/shard_map/ppermute | solution.py:17
  471.2 6.9 copy-start.3
  471.2 6.9 copy-start.7
  471.2 6.9 copy-start.15
  471.3 6.8 collective-permute-start.7
  472.7 206.2 %copy-start.10 = (f32[1,19,13,128]{3,2,1,0:T(8,128)}, f32[1,19,13,128]{3,2,1,0:T(8,128)S(1)}, u32[]{:S(2)}) copy-start(f32[1,19,13,128]{3,2,1,0:T(8,128)S(1)} %slice_add_fusion.3) | copy-start | bytes 379396
  479.9 2.4 collective-permute-start.10
  489.1 1.8 copy-start.39
  492.7 66.7 %copy-start.26 = (f32[16,343]{0,1:T(8,128)S(1)}, f32[16,343]{0,1:T(8,128)}, u32[]{:S(2)}) copy-start(f32[16,343]{0,1:T(8,128)} %copy-done.22) | copy-start | bytes 65860
  493.6 163.7 %all-gather.29.cloned.1.call-start = ((), (), s32[]{:S(2)}) async-start(), calls=%async_computation.6 | async-start | bytes 2162688 | tf_op jit(solution)/shard_map/all_gather | solution.py:91
  571.8 6.8 collective-permute-start.11
  580.1 2.2 collective-permute-start.12
  589.1 1.8 copy-start.31
  593.6 198.7 %all-gather.31.cloned.1.call-start = ((), (), s32[]{:S(2)}) async-start(), calls=%async_computation.7 | async-start | bytes 2162688 | tf_op jit(solution)/shard_map/all_gather | solution.py:91
  671.8 7.1 copy-start.4
  671.9 7.1 collective-permute-start.13
  679.4 2.1 collective-permute-start.14
  724.2 1.8 copy-start.32
  809.3 6.9 copy-start.5
  809.3 6.9 copy-start.11
  809.3 6.8 collective-permute-start.15
  816.2 1.2 copy-start.12
Sparse Core Ops, SparseCore 0:
  24.8 62.7 all-gather.16
  125.6 63.4 all-gather.18
  238.8 63.2 all-gather.20
  325.1 63.2 all-gather.24
  390.1 64.0 all-gather.22
  493.7 63.5 all-gather.26
  593.7 63.5 all-gather.28
  728.8 63.4 all-gather.30
